TPU v7x, 32 devices: a whole 2x2x4 slice. The times are simulated.
32 devices in a mesh: group: 2 (over y), head: 4 (over z), req: 4 (over x, core).
Axes of the slice: x: 2, y: 2, z: 4, core: 2. Of those that a mesh axis runs over, the one named last changes fastest.
Arguments:
- x_input: bfloat16 [128, 8, 16384], P(('group', 'req'), None, 'head'), parts along dimension 0, may hold values from -6 to 6
- z_input: bfloat16 [128, 8, 16384], P(('group', 'req'), None, 'head'), parts along dimension 0, may hold values from -6 to 6
- bc_input: bfloat16 [128, 8, 4096], P(('group', 'req')), parts along dimension 0, may hold values from -6 to 6
- dt_input: float32 [128, 8, 256], P(('group', 'req'), None, 'head'), parts along dimension 0, may hold values from -6 to 6
- conv_x_state: bfloat16 [128, 3, 16384], P(('group', 'req'), None, 'head'), parts along dimension 0, may hold values from -6 to 6
- conv_bc_state: bfloat16 [128, 3, 4096], P(('group', 'req')), parts along dimension 0, may hold values from -6 to 6
- ssm_state: bfloat16 [128, 256, 64, 256], P(('group', 'req'), 'head'), parts along dimension 0, may hold values from -6 to 6
- accepted: int32 [128], P(('group', 'req')), parts along dimension 0, may hold values from 0 to 8
- next_owner: int32 [128], P('group'), parts along dimension 0, may hold values from 0 to 3, as said below
- conv_x_weight: float32 [4, 16384], P(None, 'head'), may hold values from -3 to 3
- conv_x_bias: float32 [16384], P('head'), may hold values from -3 to 3
- conv_bc_weight: float32 [4, 4096], replicated, may hold values from -3 to 3
- conv_bc_bias: float32 [4096], replicated, may hold values from -3 to 3
- dt_bias: float32 [256], P('head'), may hold values from -3 to 0
- a_log: float32 [256], P('head'), may hold values from -4 to 1
- d_skip: float32 [256], P('head'), may hold values from 0.5 to 1.5
- norm_gain: float32 [16384], P('head'), may hold values from 0.5 to 1.5
- out_weight: bfloat16 [16384, 8192], P('head'), may hold values from -0.0625 to 0.0625
Outputs:
- mixed: bfloat16 [128, 8, 8192], P(('group', 'req'), None, 'head'), parts along dimension 0
- new_ssm_state: bfloat16 [128, 256, 64, 256], P(('group', 'req'), 'head'), parts along dimension 0
- new_conv_x_state: bfloat16 [128, 3, 16384], P(('group', 'req'), None, 'head'), parts along dimension 0
- new_conv_bc_state: bfloat16 [128, 3, 4096], P(('group', 'req')), parts along dimension 0
There are 2 independent parts, one for each index of `group`. A program takes and returns all parts, laid end to end along the dimension named above; an argument that names none is the same for every part. Nothing has to cross between parts.
Inputs may be any that keep to these rules, and one draw needn't show every extreme that they name: Every index of req is next_owner of exactly 16 requests, and at most 8 of the requests of one index of req (requests i * 16 .. i * 16 + 15) share one next_owner.
All inputs are finite; a program needn't handle non-finite values.
Results may differ from a plain program's by a relative error of at most 0.0049.
Values may be sent and summed in bfloat16 or wider, within the bound.
No kernel may reach another device: no remote copies, remote signals or barrier semaphores. Data moves between devices by JAX's collectives and lax.ppermute only.
A program may use at most 576 MiB of HBM per device.

v0:
```python
import jax
import jax.numpy as jnp
from jax import lax
from jax.sharding import PartitionSpec as P

D = 8192
H = 256
P_SIZE = 64
N = 256
G = 8
K = 4
L = 8
epsilon = 1e-05
highest = lax.Precision.HIGHEST


def conv_window(history, inputs, weight, bias_vector):
    joined = jnp.concatenate([history, inputs], axis=1)
    widened = joined.astype(jnp.float32)
    accumulated = bias_vector[None, None, :] + weight[0][None, None, :] * widened[:, 0:L, :]
    for offset in range(1, K):
        accumulated = (
            accumulated + weight[offset][None, None, :] * widened[:, offset : offset + L, :]
        )
    return (jax.nn.silu(accumulated), joined)


def on_device(
    x_input,
    z_input,
    bc_input,
    dt_input,
    conv_x_state,
    conv_bc_state,
    ssm_state,
    accepted,
    next_owner,
    conv_x_weight,
    conv_x_bias,
    conv_bc_weight,
    conv_bc_bias,
    dt_bias,
    a_log,
    d_skip,
    norm_gain,
    out_weight,
):
    local_requests = x_input.shape[0]
    local_heads = dt_input.shape[2]
    head_index = lax.axis_index("head")
    req_index = lax.axis_index("req")
    all_requests = next_owner.shape[0]
    heads_group = H // G
    x_conv, x_joined = conv_window(conv_x_state, x_input, conv_x_weight, conv_x_bias)
    bc_conv, bc_joined = conv_window(conv_bc_state, bc_input, conv_bc_weight, conv_bc_bias)
    step_size = jax.nn.softplus(dt_input + dt_bias[None, None, :])
    log_decay = -jnp.exp(a_log)[None, None, :] * step_size
    global_heads = head_index * local_heads + jnp.arange(local_heads, dtype=jnp.int32)
    group_pick = (
        global_heads[:, None] // heads_group == jnp.arange(G, dtype=jnp.int32)[None, :]
    ).astype(jnp.float32)
    b_groups = bc_conv[:, :, : G * N].reshape(local_requests, L, G, N)
    c_groups = bc_conv[:, :, G * N :].reshape(local_requests, L, G, N)
    b_heads = jnp.einsum("rlgn,hg->rlhn", b_groups, group_pick, precision=highest)
    c_heads = jnp.einsum("rlgn,hg->rlhn", c_groups, group_pick, precision=highest)
    x_heads = x_conv.reshape(local_requests, L, local_heads, P_SIZE)
    initial = ssm_state.astype(jnp.float32)
    inclusive = jnp.cumsum(log_decay, axis=1)
    before = jnp.concatenate(
        [jnp.zeros((local_requests, 1, local_heads), jnp.float32), inclusive], axis=1
    )
    positions = jnp.arange(L, dtype=jnp.int32)
    causal = positions[:, None] >= positions[None, :]
    by_head = inclusive.transpose(0, 2, 1)
    differences = by_head[:, :, :, None] - by_head[:, :, None, :]
    pair_decay = jnp.exp(jnp.where(causal[None, None], differences, -jnp.inf))
    scores = jnp.einsum("rthn,rshn->rhts", c_heads, b_heads, precision=highest)
    weights = scores * pair_decay * step_size.transpose(0, 2, 1)[:, :, None, :]
    within = jnp.einsum("rhts,rshp->rthp", weights, x_heads, precision=highest)
    carried = jnp.exp(inclusive)[:, :, :, None] * jnp.einsum(
        "rhpn,rthn->rthp", initial, c_heads, precision=highest
    )
    y_values = within + carried + d_skip[None, None, :, None] * x_heads
    count_pick = (jnp.arange(L + 1, dtype=jnp.int32)[None, :] == accepted[:, None]).astype(
        jnp.float32
    )
    reached = jnp.einsum("ra,rah->rh", count_pick, before, precision=highest)
    valid = positions[None, :] < accepted[:, None]
    exponent = jnp.where(valid[:, :, None], reached[:, None, :] - inclusive, -jnp.inf)
    token_weight = jnp.exp(exponent) * step_size
    retained = jnp.exp(reached)[:, :, None, None] * initial + jnp.einsum(
        "rsh,rshp,rshn->rhpn", token_weight, x_heads, b_heads, precision=highest
    )
    retained = retained.astype(jnp.bfloat16)
    gated = y_values.reshape(local_requests, L, local_heads * P_SIZE) * jax.nn.silu(
        z_input.astype(jnp.float32)
    )
    blocks = gated.reshape(local_requests, L, local_heads, P_SIZE)
    inverse_rms = lax.rsqrt(jnp.mean(blocks * blocks, axis=3, keepdims=True) + epsilon)
    normed = (
        (blocks * inverse_rms).reshape(local_requests, L, local_heads * P_SIZE)
        * norm_gain[None, None, :]
    ).astype(jnp.bfloat16)
    partial_terms = jnp.dot(
        normed.reshape(local_requests * L, local_heads * P_SIZE),
        out_weight,
        preferred_element_type=jnp.float32,
    )
    share_width = D // lax.axis_size("head")
    summed = lax.psum(partial_terms, "head")
    share = lax.dynamic_slice_in_dim(summed, head_index * share_width, share_width, 1)
    mixed = share.astype(jnp.bfloat16).reshape(local_requests, L, share_width)
    window_rows = jnp.arange(K - 1 + L, dtype=jnp.int32)
    row_pick = (
        window_rows[None, None, :]
        == accepted[:, None, None] + jnp.arange(K - 1, dtype=jnp.int32)[None, :, None]
    ).astype(jnp.bfloat16)
    kept_x = jnp.einsum(
        "rkt,rtc->rkc", row_pick, x_joined, preferred_element_type=jnp.float32
    ).astype(jnp.bfloat16)
    kept_bc = jnp.einsum(
        "rkt,rtc->rkc", row_pick, bc_joined, preferred_element_type=jnp.float32
    ).astype(jnp.bfloat16)
    state_flat = retained.reshape(local_requests, -1)
    conv_x_flat = kept_x.reshape(local_requests, -1)
    conv_bc_flat = kept_bc.reshape(local_requests, -1)
    request_ids = jnp.arange(all_requests, dtype=jnp.int32)
    same_owner = next_owner[:, None] == next_owner[None, :]
    earlier = request_ids[None, :] < request_ids[:, None]
    position = jnp.sum((same_owner & earlier).astype(jnp.int32), axis=1)
    slot_rows = jnp.arange(local_requests, dtype=jnp.int32)
    arrive = (
        (next_owner[None, :] == req_index) & (position[None, :] == slot_rows[:, None])
    ).astype(jnp.bfloat16)
    new_state_flat = jnp.dot(
        arrive,
        lax.all_gather(state_flat, "req", axis=0, tiled=True),
        preferred_element_type=jnp.float32,
    ).astype(jnp.bfloat16)
    new_conv_x_flat = jnp.dot(
        arrive,
        lax.all_gather(conv_x_flat, "req", axis=0, tiled=True),
        preferred_element_type=jnp.float32,
    ).astype(jnp.bfloat16)
    new_conv_bc_flat = jnp.dot(
        arrive,
        lax.all_gather(conv_bc_flat, "req", axis=0, tiled=True),
        preferred_element_type=jnp.float32,
    ).astype(jnp.bfloat16)
    new_ssm_state = new_state_flat.reshape(retained.shape)
    new_conv_x_state = new_conv_x_flat.reshape(kept_x.shape)
    new_conv_bc_state = new_conv_bc_flat.reshape(kept_bc.shape)
    return (mixed, new_ssm_state, new_conv_x_state, new_conv_bc_state)


def solution(mesh):
    placed = (
        P(("group", "req"), None, "head"),
        P(("group", "req"), None, "head"),
        P(("group", "req"), None, None),
        P(("group", "req"), None, "head"),
        P(("group", "req"), None, "head"),
        P(("group", "req"), None, None),
        P(("group", "req"), "head", None, None),
        P(("group", "req")),
        P("group"),
        P(None, "head"),
        P("head"),
        P(),
        P(),
        P("head"),
        P("head"),
        P("head"),
        P("head"),
        P("head", None),
    )
    return jax.shard_map(
        on_device,
        mesh=mesh,
        in_specs=placed,
        out_specs=(
            P(("group", "req"), None, "head"),
            P(("group", "req"), "head", None, None),
            P(("group", "req"), None, "head"),
            P(("group", "req"), None, None),
        ),
        check_vma=False,
    )
```

profile of v0, /device:TPU:0, one launch (start us, length us, event | category | flops | bytes accessed | tf_op | source)
XLA Modules:
  0.0 1015.5 jit_solution(1302443822829279630)
XLA Ops:
  7.2 0.8 iota_add_fusion
  8.1 1.3 copy.48
  9.4 2.0 convolution_convert_fusion.3
  11.4 1.0 copy.73
  12.6 0.3 copy.47
  12.9 0.8 convolution_convert_fusion.4
  13.7 1.0 copy.72
  14.9 0.1 fusion.56
  14.9 0.1 iota_compare_fusion.4
  15.0 2.6 fusion.36
  17.7 2.7 fusion.35
  20.5 0.1 reduce_window_sum.11
  20.6 0.2 fusion.46
  20.9 0.1 exponential_multiply_fusion
  21.0 7.4 divide_multiply_fusion.1
  28.4 3.0 reshape.178
  31.4 7.0 divide_multiply_fusion
  38.5 1.2 fusion.75
  39.6 1.4 copy-done.2
  41.0 2.6 broadcast_multiply_fusion
  43.7 5.8 convolution_bitcast_fusion
  49.4 72.6 %add_convert_fusion = bf16[16,64,64,256]{3,2,1,0:T(8,128)(2,1)} fusion(bf16[16,64,64,256]{3,2,1,0:T(8,128)(2,1)} %param.24, f32[16,64]{1,0:T(8,128)S(1)} %exp.40, f32[16,8,64,256]{3,2,1,0:T(8,128)} %convolution_bitcast_fusion, f32[16,8,64,64]{3,2,1,0:T(8,128)} %broadcast_multiply_fusion), kind=kOutput, calls=%fused_computation.1 | convolution fusion | flops 1677721600 | bytes 77598720 | tf_op jit(solution)/shard_map/rsh,rshp,rshn->rhpn/dot_general | solution.py:91
  122.1 31.2 %copy.70 = bf16[2,8,4096,256]{3,1,2,0:T(8,128)(2,1)} copy(bf16[2,8,4096,256]{3,2,1,0:T(8,128)(2,1)} %bitcast.78) | data formatting | bytes 67108864
  153.3 1.0 copy.53
  154.3 0.2 copy.55
  154.5 0.2 copy.51
  154.7 8.9 convolution_bitcast_fusion.1
  163.6 21.0 %fusion.1 = f32[16,64,8,8]{3,2,1,0:T(8,128)} fusion(f32[16,8,64,256]{3,2,1,0:T(8,128)S(1)} %copy-done, f32[16,8,64,256]{3,2,1,0:T(8,128)} %convolution_bitcast_fusion.1), kind=kOutput, calls=%fused_computation.5 | convolution fusion | flops 201326592 | bytes 17039360 | tf_op jit(solution)/shard_map/rthn,rshn->rhts/dot_general | solution.py:77
  184.6 16.2 %fusion.9 = f32[16,64,64,8]{2,3,1,0:T(8,128)} fusion(f32[16,64,8,8]{3,2,1,0:T(8,128)} %fusion.1, f32[16,8,64,64]{3,2,1,0:T(8,128)} %reshape.178, f32[16,64,8]{2,1,0:T(8,128)} %copy.53, f32[16,64,8]{2,1,0:T(8,128)S(1)} %copy.51, pred[8,8]{1,0:T(8,128)(4,1)S(1)} %iota_compare_fusion.7), kind=kOutput, calls=%fused_computation.16 | convolution fusion | flops 50593792 | bytes 4522048 | tf_op jit(solution)/shard_map/rhts,rshp->rthp/dot_general | solution.py:79
  200.9 35.1 %fusion.7 = f32[16,8,64,64]{3,1,2,0:T(8,128)} fusion(f32[16,64,64,8]{2,3,1,0:T(8,128)} %fusion.9, f32[16,8,64,64]{3,2,1,0:T(8,128)} %reshape.178, bf16[16,64,64,256]{3,2,1,0:T(8,128)(2,1)} %param.24, f32[16,8,64,256]{3,2,1,0:T(8,128)S(1)} %copy-done.1, f32[64]{0:T(128)S(1)} %copy-done.14, f32[16,8,64]{1,2,0:T(8,128)S(1)} %copy.55), kind=kOutput, calls=%fused_computation.14 | convolution fusion | flops 1612709888 | bytes 48267520 | tf_op jit(solution)/shard_map/rhpn,rthn->rthp/dot_general | solution.py:80
  236.0 5.4 copy.58
  241.5 4.2 reshape.181
  245.7 1.9 fusion.74
  247.6 4.7 mul.209
  252.2 3.3 reduce_sum.18
  255.6 2.6 mul.210
  258.3 4.8 mul.211
  263.0 26.6 %fusion.38 = f32[128,8192]{1,0:T(8,128)} fusion(bf16[4096,8192]{1,0:T(8,128)(2,1)} %param.35, f32[16,8,4096]{2,1,0:T(8,128)} %mul.211, f32[4096]{0:T(1024)S(1)} %copy-done.8, f32[16,8,4096]{2,1,0:T(8,128)S(1)} %reshape.181, bf16[16,8,4096]{2,1,0:T(8,128)(2,1)S(1)} %copy-done.3), kind=kOutput, calls=%fused_computation.61 | convolution fusion | flops 8594653184 | bytes 76562432 | tf_op jit(solution)/shard_map/dot_general | solution.py:104
  289.7 0.2 convert_reduce_fusion
  289.9 150.2 %all-reduce.2 = bf16[128,8192]{1,0:T(8,128)(2,1)S(1)} all-reduce(f32[128,8192]{1,0:T(8,128)} %fusion.38), channel_id=1, replica_groups=mesh['group'=2,'head'=4,'req'=4] {'head'}, use_global_device_ids=true, to_apply=%region_2.3 | all-reduce | flops 1048576 | bytes 6291456 | tf_op jit(solution)/shard_map/psum | solution.py:110
  440.1 0.8 fusion.45
  440.9 1.7 convolution_convert_fusion.1
  442.6 0.8 copy.101
  443.4 1.7 convolution_convert_fusion.2
  445.1 0.8 copy.102
  445.9 485.2 %all-gather.4.cloned.1.call-done = bf16[64,1048576]{1,0:T(8,128)(2,1)} async-done(((bf16[16,1048576]{1,0:T(8,128)(2,1)}), bf16[64,1048576]{1,0:T(8,128)(2,1)}) %all-gather.4.cloned.1.call-update) | async-done | bytes 134217744 | tf_op jit(solution)/shard_map/all_gather | solution.py:137
  931.1 54.6 %convolution_convert_fusion = bf16[16,1048576]{1,0:T(8,128)(2,1)} fusion(bf16[64,1048576]{1,0:T(8,128)(2,1)} %all-gather.4.cloned.1.call-done, s32[64]{0:T(128)S(1)} %convert_reduce_fusion, pred[64]{0:T(512)(128)(4,1)S(1)} %broadcast_compare_fusion), kind=kOutput, calls=%fused_computation | convolution fusion | flops 2164262912 | bytes 167772480 | tf_op jit(solution)/shard_map/dot_general | solution.py:135
  985.7 23.1 %copy.71 = bf16[2,8,4096,256]{3,2,1,0:T(8,128)(2,1)} copy(bf16[2,8,4096,256]{3,1,2,0:T(8,128)(2,1)} %bitcast.79) | data formatting | bytes 67108864
  (52 shorter events, 0.5 us)
Async XLA Ops:
  7.2 5.4 copy-start.6
  7.2 5.7 copy-start.4
  7.2 433.7 %all-gather.8.cloned.1.call-start = ((), (), s32[]{:S(2)}) async-start(), calls=%async_computation.2 | async-start | bytes 1966080 | tf_op jit(solution)/shard_map/all_gather | solution.py:147
  11.4 3.4 copy-start.13
  12.5 430.9 %all-gather.6.cloned.1.call-start = ((), (), s32[]{:S(2)}) async-start(), calls=%async_computation.1 | async-start | bytes 1966080 | tf_op jit(solution)/shard_map/all_gather | solution.py:142
  13.7 3.9 copy-start.5
  14.8 916.3 %all-gather.4.cloned.1.call-start = ((), (), s32[]{:S(2)}) async-start(), calls=%async_computation | async-start | bytes 167772160 | tf_op jit(solution)/shard_map/all_gather | solution.py:137
  17.7 2.8 copy-start.16
  17.7 2.8 copy-start.7
  17.7 2.8 copy-start.15
  17.7 3.1 copy-start.9
  17.7 3.2 copy-start.10
  17.7 3.4 copy-start.11
  28.4 3.0 copy-start.12
  38.5 2.6 copy-start.2
  154.7 8.9 copy-start
  184.6 16.2 %copy-start.1 = (f32[16,8,64,256]{3,2,1,0:T(8,128)S(1)}, f32[16,8,64,256]{3,2,1,0:T(8,128)}, u32[]{:S(2)}) copy-start(f32[16,8,64,256]{3,2,1,0:T(8,128)} %convolution_bitcast_fusion.1) | copy-start | bytes 25165828
  184.6 16.2 %copy-start.14 = (f32[64]{0:T(128)S(1)}, f32[64]{0:T(128)}, u32[]{:S(2)}) copy-start(f32[64]{0:T(128)} %param.33) | copy-start | bytes 772
  241.5 4.2 copy-start.3
  258.3 4.8 copy-start.8
  263.0 26.6 %copy-start.17 = (s32[64]{0:T(128)S(1)}, s32[64]{0:T(128)}, u32[]{:S(2)}) copy-start(s32[64]{0:T(128)} %param.26) | copy-start | bytes 772
Sparse Core Ops, SparseCore 0:
  12.6 22.3 all-gather.7
  37.1 19.6 all-gather.5
  153.4 777.6 all-gather.3
where the time goes:
time: 1020 us
  waiting for transfers between devices  485 us (48%)
  matrix products  247 us (24%)
  blocking collectives  150 us (15%)
  local copies, waits for them, and re-layouts  89.3 us (9%)
  other arithmetic  29 us (3%)
  between operations  14.3 us (1%)
    all_gather x1, waiting for transfers between devices, on_device(): lax.all_gather(state_flat, 'req', axis=0, tiled=True)  485 us
    psum x1, blocking collectives, on_device(): summed = lax.psum(partial_terms, 'head')  150 us
    dot_general x1, matrix products, on_device(): jnp.einsum('rsh,rshp,rshn->rhpn', token_weight, x_heads, b_heads, precisi...  72.6 us
    unnamed x42, local copies, waits for them, and re-layouts  59.5 us
    dot_general x1, matrix products, on_device(): jnp.dot(arrive, lax.all_gather(state_flat, 'req', axis=0, tiled=True), pr...  54.6 us
    dot_general x1, matrix products, on_device(): jnp.einsum('rhpn,rthn->rthp', initial, c_heads, precision=highest)  35.1 us
    dot_general x1, matrix products, on_device(): jnp.dot(normed.reshape(local_requests * L, local_heads * P_SIZE), out_wei...  26.6 us
    dot_general x1, matrix products, on_device(): scores = jnp.einsum('rthn,rshn->rhts', c_heads, b_heads, precision=highest)  21 us
  transfers between devices with their start and end apart: 3, of which 1 were waited for; matrix products, arithmetic and copies ran while one was open for 28% of the time, Pallas kernels for 0%

commit v1 on v0

--- a/solution.py
+++ b/solution.py
@@ -12,6 +12,12 @@
 L = 8
 epsilon = 1e-05
 highest = lax.Precision.HIGHEST
+
+
+def add_all(x, name):
+    terms = lax.all_gather(x, name, axis=0, tiled=False)
+    total = terms.sum(axis=0)
+    return total
 
 
 def conv_window(history, inputs, weight, bias_vector):
@@ -107,7 +113,7 @@
         preferred_element_type=jnp.float32,
     )
     share_width = D // lax.axis_size("head")
-    summed = lax.psum(partial_terms, "head")
+    summed = add_all(partial_terms, "head")
     share = lax.dynamic_slice_in_dim(summed, head_index * share_width, share_width, 1)
     mixed = share.astype(jnp.bfloat16).reshape(local_requests, L, share_width)
     window_rows = jnp.arange(K - 1 + L, dtype=jnp.int32)

time: 1020 us -> 1320 us (1.29)
  waiting for transfers between devices: 485 us -> 942 us
  blocking collectives: 150 us -> 0 us
    all_gather x1, waiting for transfers between devices: 485 us -> 766 us  [on_device(): lax.all_gather(state_flat, 'req', axis=0, tiled=True)]
    all_gather x0 -> x1, waiting for transfers between devices: none -> 176 us  [add_all(): terms = lax.all_gather(x, name, axis=0, tiled=False)]
    psum x1 -> x0, blocking collectives: 150 us -> none  [on_device(): summed = lax.psum(partial_terms, 'head')]
    unnamed x42 -> x40, local copies, waits for them, and re-layouts: 59.5 us -> 58.7 us
  transfers between devices with their start and end apart: 3 -> 4, of which waited for: 1 -> 2; matrix products, arithmetic and copies ran while one was open for 28% -> 21% of each run, Pallas kernels for 0% -> 0%
where the time goes in v1:
time: 1320 us
  waiting for transfers between devices  942 us (71%)
  matrix products  235 us (18%)
  local copies, waits for them, and re-layouts  86.5 us (7%)
  other arithmetic  38.1 us (3%)
  between operations  14.5 us (1%)
    all_gather x1, waiting for transfers between devices, on_device(): lax.all_gather(state_flat, 'req', axis=0, tiled=True)  766 us
    all_gather x1, waiting for transfers between devices, add_all(): terms = lax.all_gather(x, name, axis=0, tiled=False)  176 us
    dot_general x1, matrix products, on_device(): jnp.einsum('rsh,rshp,rshn->rhpn', token_weight, x_heads, b_heads, precisi...  72.4 us
    unnamed x40, local copies, waits for them, and re-layouts  58.7 us
    dot_general x1, matrix products, on_device(): jnp.dot(arrive, lax.all_gather(state_flat, 'req', axis=0, tiled=True), pr...  54.6 us
    dot_general x1, matrix products, on_device(): jnp.einsum('rhpn,rthn->rthp', initial, c_heads, precision=highest)  31.9 us
    dot_general x1, matrix products, on_device(): jnp.dot(normed.reshape(local_requests * L, local_heads * P_SIZE), out_wei...  26.6 us
  transfers between devices with their start and end apart: 4, of which 2 were waited for; matrix products, arithmetic and copies ran while one was open for 21% of the time, Pallas kernels for 0%

profile of v1, /device:TPU:0, one launch (start us, length us, event | category | flops | bytes accessed | tf_op | source)
XLA Modules:
  0.0 1317.0 jit_solution(12811983450559123282)
XLA Ops:
  7.2 0.8 iota_add_fusion
  8.1 1.3 copy.48
  9.4 2.0 convolution_convert_fusion.3
  11.4 1.0 copy.73
  12.6 0.3 copy.47
  12.9 0.8 convolution_convert_fusion.4
  13.7 1.0 copy.72
  14.8 0.3 all-gather.12.cloned.1.call-start
  15.1 0.1 fusion.56
  15.2 2.6 fusion.36
  17.9 2.7 fusion.35
  20.9 0.2 fusion.46
  21.1 0.1 exponential_multiply_fusion
  21.2 1.0 copy.53
  22.2 0.2 copy.55
  22.4 0.2 copy.51
  22.7 7.0 divide_multiply_fusion.1
  29.7 3.0 reshape.178
  32.7 7.1 divide_multiply_fusion
  39.8 0.2 fusion.75
  40.1 3.5 convolution_bitcast_fusion
  43.6 6.0 convolution_bitcast_fusion.1
  49.6 19.4 %fusion.1 = f32[16,64,8,8]{3,2,1,0:T(8,128)} fusion(f32[16,8,64,256]{3,2,1,0:T(8,128)S(1)} %convolution_bitcast_fusion, f32[16,8,64,256]{3,2,1,0:T(8,128)} %convolution_bitcast_fusion.1), kind=kOutput, calls=%fused_computation.5 | convolution fusion | flops 201326592 | bytes 17039360 | tf_op jit(solution)/shard_map/rthn,rshn->rhts/dot_general | solution.py:83
  69.0 14.4 %fusion.9 = f32[16,64,64,8]{2,3,1,0:T(8,128)} fusion(f32[16,64,8,8]{3,2,1,0:T(8,128)} %fusion.1, f32[16,8,64,64]{3,2,1,0:T(8,128)} %reshape.178, f32[16,64,8]{2,1,0:T(8,128)} %copy.53, f32[16,64,8]{2,1,0:T(8,128)S(1)} %copy.51, pred[8,8]{1,0:T(8,128)(4,1)S(1)} %iota_compare_fusion.7), kind=kOutput, calls=%fused_computation.16 | convolution fusion | flops 50593792 | bytes 4522048 | tf_op jit(solution)/shard_map/rhts,rshp->rthp/dot_general | solution.py:85
  83.4 31.9 %fusion.7 = f32[16,8,64,64]{3,1,2,0:T(8,128)} fusion(f32[16,64,64,8]{2,3,1,0:T(8,128)} %fusion.9, f32[16,8,64,64]{3,2,1,0:T(8,128)} %reshape.178, bf16[16,64,64,256]{3,2,1,0:T(8,128)(2,1)} %param.24, f32[16,8,64,256]{3,2,1,0:T(8,128)S(1)} %copy-done.1, f32[64]{0:T(128)S(1)} %copy-done.13, f32[16,8,64]{1,2,0:T(8,128)S(1)} %copy.55), kind=kOutput, calls=%fused_computation.14 | convolution fusion | flops 1612709888 | bytes 48267520 | tf_op jit(solution)/shard_map/rhpn,rthn->rthp/dot_general | solution.py:86
  115.3 4.9 copy.58
  120.2 3.8 reshape.181
  124.0 1.9 fusion.74
  125.9 4.6 mul.209
  130.5 3.3 reduce_sum.27
  133.8 2.6 mul.210
  136.5 4.8 mul.211
  141.3 26.6 %fusion.38 = f32[128,8192]{1,0:T(8,128)} fusion(bf16[4096,8192]{1,0:T(8,128)(2,1)} %param.35, f32[16,8,4096]{2,1,0:T(8,128)} %mul.211, f32[4096]{0:T(1024)S(1)} %copy-done.7, f32[16,8,4096]{2,1,0:T(8,128)S(1)} %reshape.181, bf16[16,8,4096]{2,1,0:T(8,128)(2,1)S(1)} %copy-done.2), kind=kOutput, calls=%fused_computation.61 | convolution fusion | flops 8594653184 | bytes 76562432 | tf_op jit(solution)/shard_map/dot_general | solution.py:110
  168.0 4.2 broadcast_multiply_fusion
  172.2 72.4 %add_convert_fusion = bf16[16,64,64,256]{3,2,1,0:T(8,128)(2,1)} fusion(bf16[16,64,64,256]{3,2,1,0:T(8,128)(2,1)} %param.24, f32[16,64]{1,0:T(8,128)S(1)} %exp.40, f32[16,8,64,256]{3,2,1,0:T(8,128)} %copy-done, f32[16,8,64,64]{3,2,1,0:T(8,128)} %broadcast_multiply_fusion), kind=kOutput, calls=%fused_computation.1 | convolution fusion | flops 1677721600 | bytes 77598720 | tf_op jit(solution)/shard_map/rsh,rshp,rshn->rhpn/dot_general | solution.py:97
  244.6 31.2 %copy.70 = bf16[2,8,4096,256]{3,1,2,0:T(8,128)(2,1)} copy(bf16[2,8,4096,256]{3,2,1,0:T(8,128)(2,1)} %bitcast.79) | data formatting | bytes 67108864
  275.8 0.6 copy-done.16
  276.5 0.2 convert_reduce_fusion
  276.7 1.7 convolution_convert_fusion.1
  278.4 0.8 copy.101
  279.2 1.7 convolution_convert_fusion.2
  280.9 0.8 copy.102
  281.7 175.9 %all-gather.12.cloned.1.call-done = f32[512,8192]{1,0:T(8,128)} async-done(((f32[128,8192]{1,0:T(8,128)}), f32[512,8192]{1,0:T(8,128)}) %all-gather.12.cloned.1.call-update) | async-done | bytes 16777232 | tf_op jit(solution)/shard_map/all_gather | solution.py:18
  457.6 7.8 reduce_sum.28
  465.4 0.8 fusion.45
  466.2 766.1 %all-gather.6.cloned.1.call-done = bf16[64,1048576]{1,0:T(8,128)(2,1)} async-done(((bf16[16,1048576]{1,0:T(8,128)(2,1)}), bf16[64,1048576]{1,0:T(8,128)(2,1)}) %all-gather.6.cloned.1.call-update) | async-done | bytes 134217744 | tf_op jit(solution)/shard_map/all_gather | solution.py:143
  1232.3 54.6 %convolution_convert_fusion = bf16[16,1048576]{1,0:T(8,128)(2,1)} fusion(bf16[64,1048576]{1,0:T(8,128)(2,1)} %all-gather.6.cloned.1.call-done, s32[64]{0:T(128)S(1)} %convert_reduce_fusion, pred[64]{0:T(512)(128)(4,1)S(1)} %broadcast_compare_fusion), kind=kOutput, calls=%fused_computation | convolution fusion | flops 2164262912 | bytes 167772480 | tf_op jit(solution)/shard_map/dot_general | solution.py:141
  1286.9 23.1 %copy.71 = bf16[2,8,4096,256]{3,2,1,0:T(8,128)(2,1)} copy(bf16[2,8,4096,256]{3,1,2,0:T(8,128)(2,1)} %bitcast.80) | data formatting | bytes 67108864
  (53 shorter events, 0.6 us)
Async XLA Ops:
  7.2 5.4 copy-start.5
  7.2 5.7 copy-start.3
  7.2 269.5 %all-gather.10.cloned.1.call-start = ((), (), s32[]{:S(2)}) async-start(), calls=%async_computation.2 | async-start | bytes 1966080 | tf_op jit(solution)/shard_map/all_gather | solution.py:153
  11.4 3.7 copy-start.12
  12.5 266.7 %all-gather.8.cloned.1.call-start = ((), (), s32[]{:S(2)}) async-start(), calls=%async_computation.1 | async-start | bytes 1966080 | tf_op jit(solution)/shard_map/all_gather | solution.py:148
  13.7 4.1 copy-start.4
  14.8 442.8 %all-gather.12.cloned.1.call-start = ((), (), s32[]{:S(2)}) async-start(), calls=%async_computation.3 | async-start | bytes 20971520 | tf_op jit(solution)/shard_map/all_gather | solution.py:18
  17.9 2.8 copy-start.15
  17.9 2.8 copy-start.8
  17.9 2.8 copy-start.9
  17.9 2.9 copy-start.6
  17.9 2.9 copy-start.14
  17.9 4.8 copy-start.10
  29.7 3.0 copy-start.11
  43.5 6.0 copy-start
  69.0 14.4 %copy-start.1 = (f32[16,8,64,256]{3,2,1,0:T(8,128)S(1)}, f32[16,8,64,256]{3,2,1,0:T(8,128)}, u32[]{:S(2)}) copy-start(f32[16,8,64,256]{3,2,1,0:T(8,128)} %convolution_bitcast_fusion.1) | copy-start | bytes 25165828
  69.0 14.4 %copy-start.13 = (f32[64]{0:T(128)S(1)}, f32[64]{0:T(128)}, u32[]{:S(2)}) copy-start(f32[64]{0:T(128)} %param.33) | copy-start | bytes 772
  120.2 3.8 copy-start.2
  136.5 4.8 copy-start.7
  167.9 1064.4 %all-gather.6.cloned.1.call-start = ((), (), s32[]{:S(2)}) async-start(), calls=%async_computation | async-start | bytes 167772160 | tf_op jit(solution)/shard_map/all_gather | solution.py:143
  275.8 0.7 copy-start.16
Sparse Core Ops, SparseCore 0:
  12.6 22.3 all-gather.9
  37.1 19.6 all-gather.7
  168.1 289.4 all-gather.11
  459.0 773.2 all-gather.5
